TPU v7x, 512 devices: a whole 4x4x16 slice. The times are simulated.
512 devices in a mesh: row: 32 (over z, core), col: 16 (over y, x).
Axes of the slice: x: 4, y: 4, z: 16, core: 2. Of those that a mesh axis runs over, the one named last changes fastest.
Arguments:
- tokens: bfloat16 [512, 8192], P('row', 'col'), may hold values from -6 to 6
- out_grad: bfloat16 [512, 8192], P('row', 'col'), may hold values from -1.5 to 1.5
- gate_weight: bfloat16 [8192, 16384], P('col', 'row'), may hold values from -0.0625 to 0.0625
- up_weight: bfloat16 [8192, 16384], P('col', 'row'), may hold values from -0.0625 to 0.0625
- down_weight: bfloat16 [16384, 8192], P('row', 'col'), may hold values from -0.046875 to 0.046875
Outputs:
- input_grad: bfloat16 [512, 8192], P('row', 'col')
- gate_weight_grad: bfloat16 [8192, 16384], P('col', 'row')
- up_weight_grad: bfloat16 [8192, 16384], P('col', 'row')
- down_weight_grad: bfloat16 [16384, 8192], P('row', 'col')
All inputs are finite; a program needn't handle non-finite values.
Results may differ from a plain program's by a relative error of at most 0.005.
Values may be sent and summed in bfloat16 or wider, within the bound.
No kernel may reach another device: no remote copies, remote signals or barrier semaphores. Data moves between devices by JAX's collectives and lax.ppermute only.
A program may use at most 64 MiB of HBM per device.

v0:
```python
import jax
import jax.numpy as jnp
from jax import lax
from jax.sharding import PartitionSpec as P


def pointwise(gate, up, hidden_grad):
    sig = jax.nn.sigmoid(gate)
    act = gate * sig
    hidden = (act * up).astype(jnp.bfloat16)
    gate_grad = (hidden_grad * up * sig * (1.0 + gate * (1.0 - sig))).astype(jnp.bfloat16)
    up_grad = (hidden_grad * act).astype(jnp.bfloat16)
    return (hidden, gate_grad, up_grad)


def body(tokens, out_grad, gate_weight, up_weight, down_weight):
    rows_all, grads_all = (
        lax.all_gather(tokens, "row", axis=0, tiled=True),
        lax.all_gather(out_grad, "row", axis=0, tiled=True),
    )
    contract_cols = (((1,), (1,)), ((), ()))
    contract_rows = (((0,), (0,)), ((), ()))
    gate_part = jnp.dot(rows_all, gate_weight, preferred_element_type=jnp.float32)
    up_part = jnp.dot(rows_all, up_weight, preferred_element_type=jnp.float32)
    grad_part = lax.dot_general(
        grads_all, down_weight, contract_cols, preferred_element_type=jnp.float32
    )
    gate, up, hidden_grad = lax.psum((gate_part, up_part, grad_part), "col")
    hidden, gate_grad, up_grad = pointwise(gate, up, hidden_grad)
    gate_weight_grad = lax.dot_general(
        rows_all, gate_grad, contract_rows, preferred_element_type=jnp.float32
    ).astype(jnp.bfloat16)
    up_weight_grad = lax.dot_general(
        rows_all, up_grad, contract_rows, preferred_element_type=jnp.float32
    ).astype(jnp.bfloat16)
    down_weight_grad = lax.dot_general(
        hidden, grads_all, contract_rows, preferred_element_type=jnp.float32
    ).astype(jnp.bfloat16)
    total = lax.dot_general(
        gate_grad, gate_weight, contract_cols, preferred_element_type=jnp.float32
    )
    input_grad = lax.psum_scatter(
        total
        + lax.dot_general(up_grad, up_weight, contract_cols, preferred_element_type=jnp.float32),
        "row",
        scatter_dimension=0,
        tiled=True,
    )
    return (input_grad.astype(jnp.bfloat16), gate_weight_grad, up_weight_grad, down_weight_grad)


def solution(mesh):
    return jax.shard_map(
        body,
        mesh=mesh,
        in_specs=(
            P("row", "col"),
            P("row", "col"),
            P("col", "row"),
            P("col", "row"),
            P("row", "col"),
        ),
        out_specs=(P("row", "col"), P("col", "row"), P("col", "row"), P("row", "col")),
        check_vma=False,
    )
```

profile of v0, /device:TPU:2, one launch (start us, length us, event | category | flops | bytes accessed | tf_op | source)
XLA Modules:
  0.0 323.2 jit_solution(6330237184376752438)
XLA Ops:
  7.2 0.0 copy-start
  7.2 0.0 all-reduce.3.cloned.1.call-start
  7.2 38.0 %all_gather.7 = bf16[512,512]{1,0:T(8,128)(2,1)S(1)} all-gather(bf16[16,512]{1,0:T(8,128)(2,1)} %param.5), channel_id=1, replica_groups=mesh['row'=32,'col'=16] {'row'}, dimensions={0}, use_global_device_ids=true | all-gather | bytes 540672 | tf_op jit(solution)/shard_map/all_gather | solution.py:18
  45.3 28.5 %all_gather.6 = bf16[512,512]{1,0:T(8,128)(2,1)S(1)} all-gather(bf16[16,512]{1,0:T(8,128)(2,1)S(1)} %copy-done.4), channel_id=1, replica_groups=mesh['row'=32,'col'=16] {'row'}, dimensions={0}, use_global_device_ids=true | all-gather | bytes 540672 | tf_op jit(solution)/shard_map/all_gather | solution.py:19
  73.8 0.0 copy-done
  73.8 1.4 fusion.7
  75.2 1.4 fusion.6
  76.7 1.4 fusion.5
  78.1 0.0 all-reduce.3.cloned.1.call-update
  78.1 0.0 reduce-scatter.2.cloned.1.call-start
  78.2 122.5 %all-reduce.3.cloned.1.call-done = (f32[512,512]{1,0:T(8,128)}, f32[512,512]{1,0:T(8,128)}, f32[512,512]{1,0:T(8,128)}) async-done(((f32[512,512]{1,0:T(8,128)}, f32[512,512]{1,0:T(8,128)}, f32[512,512]{1,0:T(8,128)}), (f32[512,512]{1,0:T(8,128)}, f32[512,512]{1,0:T(8,128)}, f32[512,512]{1,0:T(8,128)})) %all-reduce.3.cloned.1.call-update) | async-done | bytes 3145744 | tf_op jit(solution)/shard_map/psum | solution.py:28
  200.7 2.5 multiply_convert_fusion.1
  203.1 0.5 fusion.8
  203.6 1.5 convolution_add_fusion
  205.1 0.0 reduce-scatter.2.cloned.1.call-update
  205.1 0.5 fusion
  205.5 1.0 copy.9
  206.6 0.5 fusion.1
  207.0 0.0 copy-start.2
  207.0 1.0 copy.10
  208.0 0.4 copy-done.2
  208.4 2.5 convolution_convert_fusion
  211.0 104.1 %reduce-scatter.2.cloned.1.call-done = f32[16,512]{1,0:T(8,128)} async-done(((f32[512,512]{1,0:T(8,128)}), f32[16,512]{1,0:T(8,128)}) %reduce-scatter.2.cloned.1.call-update) | async-done | bytes 32784 | tf_op jit(solution)/shard_map/reduce_scatter | solution.py:42
  315.0 1.4 convert_element_type.29
  (6 shorter events, 0.0 us)
Async XLA Ops:
  7.2 66.6 %copy-start = (bf16[512,512]{1,0:T(8,128)(2,1)S(1)}, bf16[512,512]{1,0:T(8,128)(2,1)}, u32[]{:S(2)}) copy-start(bf16[512,512]{1,0:T(8,128)(2,1)} %param.7) | copy-start | bytes 1572868
  7.2 38.1 %copy-start.4 = (bf16[16,512]{1,0:T(8,128)(2,1)S(1)}, bf16[16,512]{1,0:T(8,128)(2,1)}, u32[]{:S(2)}) copy-start(bf16[16,512]{1,0:T(8,128)(2,1)} %param.6) | copy-start | bytes 49156
  7.2 193.5 %all-reduce.3.cloned.1.call-start = ((), (), s32[]{:S(2)}) async-start(), calls=%async_computation.2 | async-start | bytes 6291456 | tf_op jit(solution)/shard_map/psum | solution.py:28
  73.8 1.4 copy-start.1
  75.2 1.5 copy-start.3
  78.1 236.9 %reduce-scatter.2.cloned.1.call-start = ((), (), s32[]{:S(2)}) async-start(), calls=%async_computation.1 | async-start | bytes 1081344 | tf_op jit(solution)/shard_map/reduce_scatter | solution.py:42
  207.0 1.4 copy-start.2
Sparse Core Ops, SparseCore 0:
  78.2 122.3 all-reduce.2
  205.2 109.7 reduce-scatter.1
where the time goes:
time: 324 us; the launch traced here: 323 us
  waiting for transfers between devices  227 us (70%)
  blocking collectives  66.5 us (21%)
  between operations  14.1 us (4%)
  matrix products  9.67 us (3%)
  other arithmetic  3.82 us (1%)
    psum x1, waiting for transfers between devices, body(): gate, up, hidden_grad = lax.psum((gate_part, up_part, grad_part), 'col')  122 us
    reduce_scatter x1, waiting for transfers between devices, body(): lax.psum_scatter(total + lax.dot_general(up_grad, up_weight, contract_col...  104 us
    all_gather x1, blocking collectives, body(): lax.all_gather(tokens, 'row', axis=0, tiled=True)  38 us
    all_gather x1, blocking collectives, body(): lax.all_gather(out_grad, 'row', axis=0, tiled=True)  28.5 us
  transfers between devices with their start and end apart: 2, of which 2 were waited for; matrix products, arithmetic and copies ran while one was open for 2% of the time, Pallas kernels for 0%

commit v1 on v0

--- a/solution.py
+++ b/solution.py
@@ -2,6 +2,12 @@
 import jax.numpy as jnp
 from jax import lax
 from jax.sharding import PartitionSpec as P
+
+
+def press_patches(a_name, work_x):
+    return jnp.concatenate(
+        lax.all_to_all(jnp.stack([work_x] * lax.psum(1, a_name), 0), a_name, 0, 0), axis=0
+    )
 
 
 def pointwise(gate, up, hidden_grad):
@@ -15,7 +21,7 @@
 
 def body(tokens, out_grad, gate_weight, up_weight, down_weight):
     rows_all, grads_all = (
-        lax.all_gather(tokens, "row", axis=0, tiled=True),
+        press_patches("row", tokens),
         lax.all_gather(out_grad, "row", axis=0, tiled=True),
     )
     contract_cols = (((1,), (1,)), ((), ()))

time: 324 us -> 329 us (1.015)
  starting transfers between devices: 0.08 us -> 15.7 us
  blocking collectives: 66.5 us -> 51.1 us
    all_gather x1 -> x0, blocking collectives: 38 us -> none  [body(): lax.all_gather(tokens, 'row', axis=0, tiled=True)]
    all_gather x1, blocking collectives: 28.5 us -> 51.1 us  [body(): lax.all_gather(out_grad, 'row', axis=0, tiled=True)]
    all_to_all x0 -> x1, starting transfers between devices: none -> 15.6 us  [press_patches(): lax.all_to_all(jnp.stack([work_x] * lax.psum(1, a_name), 0), a_name, 0, 0)]
  transfers between devices with their start and end apart: 2 -> 3, of which waited for: 2 -> 2; matrix products, arithmetic and copies ran while one was open for 2% -> 2% of each run, Pallas kernels for 0% -> 0%
where the time goes in v1:
time: 329 us; the launch traced here: 328 us
  waiting for transfers between devices  230 us (70%)
  blocking collectives  51.1 us (16%)
  starting transfers between devices  15.7 us (5%)
  between operations  14.1 us (4%)
  matrix products  9.68 us (3%)
  local copies, waits for them, and re-layouts  4.06 us (1%)
  other arithmetic  3.82 us (1%)
    psum x1, waiting for transfers between devices, body(): gate, up, hidden_grad = lax.psum((gate_part, up_part, grad_part), 'col')  126 us
    reduce_scatter x1, waiting for transfers between devices, body(): lax.psum_scatter(total + lax.dot_general(up_grad, up_weight, contract_col...  104 us
    all_gather x1, blocking collectives, body(): lax.all_gather(out_grad, 'row', axis=0, tiled=True)  51.1 us
    all_to_all x1, starting transfers between devices, press_patches(): lax.all_to_all(jnp.stack([work_x] * lax.psum(1, a_name), 0), a_name, 0, 0)  15.6 us
  transfers between devices with their start and end apart: 3, of which 2 were waited for; matrix products, arithmetic and copies ran while one was open for 2% of the time, Pallas kernels for 0%

profile of v1, /device:TPU:2, one launch (start us, length us, event | category | flops | bytes accessed | tf_op | source)
XLA Modules:
  0.0 328.1 jit_solution(4223333563694570269)
XLA Ops:
  7.2 0.0 copy-start
  7.2 1.6 stack.2
  8.8 15.6 %all-to-all-start = ((bf16[32,16,512]{2,1,0:T(8,128)(2,1)}), bf16[32,16,512]{2,1,0:T(8,128)(2,1)S(1)}, u32[]{:S(2)}, u32[]{:S(2)}) async-start(bf16[32,16,512]{2,1,0:T(8,128)(2,1)} %stack.2), calls=%async_computation | async-start | bytes 1048576 | tf_op jit(solution)/shard_map/all_to_all | solution.py:9
  24.4 0.0 copy-start.3
  24.4 0.0 all-reduce.3.cloned.1.call-start
  24.5 51.1 %all_gather.3 = bf16[512,512]{1,0:T(8,128)(2,1)S(1)} all-gather(bf16[16,512]{1,0:T(8,128)(2,1)S(1)} %copy-done.4), channel_id=1, replica_groups=mesh['row'=32,'col'=16] {'row'}, dimensions={0}, use_global_device_ids=true | all-gather | bytes 540672 | tf_op jit(solution)/shard_map/all_gather | solution.py:25
  75.6 1.4 fusion.5
  77.1 1.4 fusion.7
  78.5 1.4 fusion.6
  79.9 0.0 all-reduce.3.cloned.1.call-update
  80.0 0.0 reduce-scatter.2.cloned.1.call-start
  80.0 125.5 %all-reduce.3.cloned.1.call-done = (f32[512,512]{1,0:T(8,128)}, f32[512,512]{1,0:T(8,128)}, f32[512,512]{1,0:T(8,128)}) async-done(((f32[512,512]{1,0:T(8,128)}, f32[512,512]{1,0:T(8,128)}, f32[512,512]{1,0:T(8,128)}), (f32[512,512]{1,0:T(8,128)}, f32[512,512]{1,0:T(8,128)}, f32[512,512]{1,0:T(8,128)})) %all-reduce.3.cloned.1.call-update) | async-done | bytes 3145744 | tf_op jit(solution)/shard_map/psum | solution.py:34
  205.5 2.5 multiply_convert_fusion.1
  208.0 0.5 fusion.8
  208.5 1.5 convolution_add_fusion
  209.9 0.0 reduce-scatter.2.cloned.1.call-update
  209.9 0.5 fusion
  210.4 1.0 copy.9
  211.4 0.5 fusion.1
  211.9 1.0 copy.10
  212.9 0.4 copy-done.2
  213.3 2.5 convolution_convert_fusion
  215.8 104.1 %reduce-scatter.2.cloned.1.call-done = f32[16,512]{1,0:T(8,128)} async-done(((f32[512,512]{1,0:T(8,128)}), f32[16,512]{1,0:T(8,128)}) %reduce-scatter.2.cloned.1.call-update) | async-done | bytes 32784 | tf_op jit(solution)/shard_map/reduce_scatter | solution.py:48
  319.9 1.4 convert_element_type.29
  (8 shorter events, 0.0 us)
Async XLA Ops:
  7.2 69.9 %copy-start = (bf16[512,512]{1,0:T(8,128)(2,1)S(1)}, bf16[512,512]{1,0:T(8,128)(2,1)}, u32[]{:S(2)}) copy-start(bf16[512,512]{1,0:T(8,128)(2,1)} %param.7) | copy-start | bytes 1572868
  8.8 15.7 %copy-start.4 = (bf16[16,512]{1,0:T(8,128)(2,1)S(1)}, bf16[16,512]{1,0:T(8,128)(2,1)}, u32[]{:S(2)}) copy-start(bf16[16,512]{1,0:T(8,128)(2,1)} %param.6) | copy-start | bytes 49156
  8.8 68.2 %all-to-all-start = ((bf16[32,16,512]{2,1,0:T(8,128)(2,1)}), bf16[32,16,512]{2,1,0:T(8,128)(2,1)S(1)}, u32[]{:S(2)}, u32[]{:S(2)}) async-start(bf16[32,16,512]{2,1,0:T(8,128)(2,1)} %stack.2), calls=%async_computation | async-start | bytes 1048576 | tf_op jit(solution)/shard_map/all_to_all | solution.py:9
  24.4 51.2 %copy-start.3 = (bf16[512,512]{1,0:T(8,128)(2,1)S(1)}, bf16[512,512]{1,0:T(8,128)(2,1)}, u32[]{:S(2)}) copy-start(bf16[512,512]{1,0:T(8,128)(2,1)} %param.9) | copy-start | bytes 1572868
  24.4 181.1 %all-reduce.3.cloned.1.call-start = ((), (), s32[]{:S(2)}) async-start(), calls=%async_computation.3 | async-start | bytes 6291456 | tf_op jit(solution)/shard_map/psum | solution.py:34
  77.1 1.4 copy-start.1
  80.0 240.0 %reduce-scatter.2.cloned.1.call-start = ((), (), s32[]{:S(2)}) async-start(), calls=%async_computation.2 | async-start | bytes 1081344 | tf_op jit(solution)/shard_map/reduce_scatter | solution.py:48
  211.9 1.4 copy-start.2
Sparse Core Ops, SparseCore 0:
  80.1 125.4 all-reduce.2
  210.1 109.8 reduce-scatter.1
